TPU v7x, 128 devices: a whole 4x4x4 slice. The times are simulated.
128 devices in a mesh: dp: 16 (over y, z_lo, core), tensor: 8 (over z_hi, x).
Axes of the slice: x: 4, y: 4, z: 4 (z_hi: 2, z_lo: 2; z = z_hi * 2 + z_lo), core: 2. Of those that a mesh axis runs over, the one named last changes fastest.
Arguments:
- stream: bfloat16 [16384, 2048], P(('dp', 'tensor')), may hold values from -6 to 6
- segment: int32 [16384], P('dp'), may hold values from -1 to 16383, as said below
- position: int32 [16384], P('dp'), may hold values from 0 to 4606, as said below
- w_qkv: bfloat16 [3, 2048, 2048], P(None, 'dp', 'tensor'), may hold values from -0.5 to 0.5
- w_out: bfloat16 [2048, 2048], P('tensor', 'dp'), may hold values from -0.125 to 0.125
- w_gate_up: bfloat16 [2, 2048, 8192], P(None, 'dp', 'tensor'), may hold values from -0.125 to 0.125
- w_down: bfloat16 [8192, 2048], P('tensor', 'dp'), may hold values from -0.0625 to 0.0625
- page_table: int32 [1024], P('dp'), may hold values from 0 to 1023, as said below
Outputs:
- layer_out: bfloat16 [16384, 2048], P(('dp', 'tensor'))
- kv_cache: bfloat16 [1024, 2, 16, 2048], P('dp', None, None, 'tensor')
Inputs may be any that keep to these rules, and one draw needn't show every extreme that they name: `segment`: each group's tokens form prompts of 64 to 512 tokens with distinct numbers, laid one after another, followed by padding -1 at the end of the group's stream; some prompt has 512 tokens in every group. Within a prompt positions rise by one from a first position below 4096; padding has position 0; in every group some prompt of 512 tokens starts at 4095. `page_table`: A permutation of all 1024 page ids. Among the 64 blocks of one request group, exactly 4 fall into each of the ranges o * 64 to (o + 1) * 64 - 1.
All inputs are finite; a program needn't handle non-finite values.
Results may differ from a plain program's by a relative error of at most 0.015.
Values may be sent and summed in bfloat16 or wider, within the bound.
No kernel may reach another device: no remote copies, remote signals or barrier semaphores. Data moves between devices by JAX's collectives and lax.ppermute only.
A program may use at most 128 MiB of HBM per device.

v0:
```python
import math
import jax
import jax.numpy as jnp
from jax import lax
from jax.sharding import PartitionSpec as P

HD = 128


def layer_norm(values):
    values = values.astype(jnp.float32)
    center = values - jnp.mean(values, axis=-1, keepdims=True)
    spread = jnp.mean(center * center, axis=-1, keepdims=True)
    return center * lax.rsqrt(spread + 1e-05)


def rotate(values, position):
    half = values.shape[-1] // 2
    freq = 10000.0 ** (-jnp.arange(half, dtype=jnp.float32) * 2.0 / values.shape[-1])
    angle = position.astype(jnp.float32)[:, None] * freq[None, :]
    cosine = jnp.cos(angle)[:, None, :]
    sine = jnp.sin(angle)[:, None, :]
    first = values[..., :half]
    second = values[..., half:]
    return jnp.concatenate(
        [first * cosine - second * sine, second * cosine + first * sine], axis=-1
    )


def row_folder(source, piece):
    return jnp.einsum("td,cdf->ctf", source, piece, preferred_element_type=jnp.float32)


def attend(query, keys, values, segment):
    tokens = query.shape[0]
    block = min(512, tokens)
    scale = 1.0 / math.sqrt(HD)
    order = jnp.arange(tokens)
    outputs = []
    for first in range(0, tokens, block):
        last = first + block
        scores = (
            jnp.einsum(
                "qhd,khd->hqk", query[first:last], keys[:last], preferred_element_type=jnp.float32
            )
            * scale
        )
        allowed = (segment[first:last, None] == segment[None, :last]) & (
            order[None, :last] <= order[first:last, None]
        )
        top = jnp.max(jnp.where(allowed[None], scores, -1e30), axis=-1, keepdims=True)
        weights = jnp.exp(jnp.where(allowed[None], scores - top, -1e30))
        total = jnp.sum(weights, axis=-1)
        mixed = jnp.einsum(
            "hqk,khd->qhd",
            weights.astype(jnp.bfloat16),
            values[:last],
            preferred_element_type=jnp.float32,
        )
        outputs.append((mixed / jnp.transpose(total)[:, :, None]).astype(jnp.bfloat16))
    return jnp.concatenate(outputs, axis=0).reshape(tokens, -1)


def write_cache(keys, values, page_table):
    tokens = keys.shape[0]
    width = keys.shape[1] * keys.shape[2]
    pages = page_table.shape[0]
    page_size = tokens // pages
    owners = lax.axis_size("dp")
    per_owner = pages // owners
    stacked = jnp.stack([keys.reshape(tokens, width), values.reshape(tokens, width)], axis=0)
    stacked = stacked.reshape(2, pages, page_size, width).transpose(1, 0, 2, 3)
    order = jnp.argsort(page_table // pages, stable=True)
    outgoing = stacked[order].reshape(owners, per_owner, 2, page_size, width)
    outgoing_ids = page_table[order].reshape(owners, per_owner)
    arrived, arrived_ids = (
        lax.all_to_all(outgoing, "dp", split_axis=0, concat_axis=0, tiled=True),
        lax.all_to_all(outgoing_ids, "dp", split_axis=0, concat_axis=0, tiled=True),
    )
    local = (arrived_ids - lax.axis_index("dp") * pages).reshape(-1)
    empty = jnp.zeros((pages, 2, page_size, width), jnp.bfloat16)
    return empty.at[local].set(arrived.reshape(pages, 2, page_size, width))


def body(stream, segment, position, w_qkv, w_out, w_gate_up, w_down, page_table):
    tok_group = segment.shape[0]
    share_rows = stream.shape[0]
    full_stream = lax.all_gather(stream, "tensor", axis=0, tiled=True)
    normed = layer_norm(full_stream).astype(jnp.bfloat16)
    local_heads = w_qkv.shape[2] // HD
    projected = row_folder(normed, lax.all_gather(w_qkv, "dp", axis=1, tiled=True))
    query = rotate(projected[0].reshape(tok_group, local_heads, HD), position).astype(jnp.bfloat16)
    keys = rotate(projected[1].reshape(tok_group, local_heads, HD), position).astype(jnp.bfloat16)
    values = projected[2].reshape(tok_group, local_heads, HD).astype(jnp.bfloat16)
    context = attend(query, keys, values, segment)
    attn_part = jnp.dot(
        context, lax.all_gather(w_out, "dp", axis=1, tiled=True), preferred_element_type=jnp.float32
    )
    attn_whole = lax.psum(attn_part.astype(jnp.bfloat16), "tensor").astype(jnp.float32)
    mid = (full_stream.astype(jnp.float32) + attn_whole).astype(jnp.bfloat16)
    normed2 = layer_norm(mid).astype(jnp.bfloat16)
    gate_up = row_folder(normed2, lax.all_gather(w_gate_up, "dp", axis=1, tiled=True))
    hidden = (jax.nn.silu(gate_up[0]) * gate_up[1]).astype(jnp.bfloat16)
    mlp_part = jnp.dot(
        hidden, lax.all_gather(w_down, "dp", axis=1, tiled=True), preferred_element_type=jnp.float32
    )
    mlp_whole = lax.psum(mlp_part.astype(jnp.bfloat16), "tensor").astype(jnp.float32)
    result = (mid.astype(jnp.float32) + mlp_whole).astype(jnp.bfloat16)
    layer_out = lax.dynamic_slice_in_dim(
        result, lax.axis_index("tensor") * share_rows, share_rows, 0
    )
    kv_cache = write_cache(keys, values, page_table)
    return (layer_out, kv_cache)


def solution(mesh):
    return jax.shard_map(
        body,
        mesh=mesh,
        in_specs=(
            P(("dp", "tensor"), None),
            P("dp"),
            P("dp"),
            P(None, "dp", "tensor"),
            P("tensor", "dp"),
            P(None, "dp", "tensor"),
            P("tensor", "dp"),
            P("dp"),
        ),
        out_specs=(P(("dp", "tensor"), None), P("dp", None, None, "tensor")),
        check_vma=False,
    )
```

profile of v0, /device:TPU:1, one launch (start us, length us, event | category | flops | bytes accessed | tf_op | source)
XLA Modules:
  0.0 515.2 jit_solution(17798327678414374484)
XLA Ops:
  7.2 0.7 all-gather.6.cloned.1.call-update
  7.9 1.7 copy.27
  9.8 0.7 all-gather.10.cloned.1.call-update
  10.5 0.7 convert_element_type.76
  11.2 0.8 fusion.83
  12.0 1.9 multiply_cosine_fusion
  13.9 0.3 compare_and_fusion
  14.2 2.1 fusion.35
  16.2 68.2 %all-gather.6.cloned.1.call-done = bf16[1024,2048]{1,0:T(8,128)(2,1)} async-done(((bf16[128,2048]{1,0:T(8,128)(2,1)}), bf16[1024,2048]{1,0:T(8,128)(2,1)}) %all-gather.6.cloned.1.call-update) | async-done | bytes 4194320 | tf_op jit(solution)/shard_map/all_gather | solution.py:88
  84.4 3.0 convert_reduce_fusion
  87.4 0.5 copy-done.2
  87.9 1.2 fusion.4
  89.1 37.2 %all-gather.8.cloned.1.call-done = bf16[3,2048,256]{1,2,0:T(8,128)(2,1)} async-done(((bf16[3,128,256]{1,2,0:T(8,128)(2,1)}), bf16[3,2048,256]{1,2,0:T(8,128)(2,1)}) %all-gather.8.cloned.1.call-update) | async-done | bytes 3145744 | tf_op jit(solution)/shard_map/all_gather | solution.py:91
  126.3 7.3 %fusion.38 = f32[3,1024,256]{1,2,0:T(8,128)S(1)} fusion(bf16[3,2048,256]{1,2,0:T(8,128)(2,1)} %all-gather.8.cloned.1.call-done, bf16[1024,2048]{1,0:T(8,128)(2,1)} %all-gather.6.cloned.1.call-done, f32[1024]{0:T(1024)S(1)} %add_rsqrt_fusion.1, f32[1024]{0:T(1024)S(1)} %broadcast_multiply_fusion.1), kind=kOutput, calls=%fused_computation.47 | convolution fusion | flops 3229614080 | bytes 10493952 | tf_op jit(solution)/shard_map/td,cdf->ctf/dot_general | solution.py:31
  133.6 0.2 fusion.80
  133.9 0.9 slice.112
  134.8 1.0 fusion.81
  135.8 1.4 copy.41
  137.2 2.4 copy.42
  139.5 1.1 fusion.82
  140.6 1.4 copy.39
  142.0 2.4 copy.40
  144.4 1.6 multiply_subtract_fusion
  145.9 0.3 maximum_convert_fusion
  146.3 0.3 subtract_convert_fusion
  146.6 0.8 copy-done.7
  147.3 0.5 fusion.60
  147.9 1.3 copy-done.6
  149.2 1.1 fusion.85
  150.3 3.4 fusion.48
  153.7 3.9 fusion.84
  157.6 2.5 fusion.49
  160.1 1.8 all-gather.10.cloned.1.call-done
  161.9 4.5 convolution_convert_fusion
  166.5 0.5 all-gather.12.cloned.1.call-update
  167.1 0.5 all-gather.14.cloned.1.call-update
  167.6 0.3 all-reduce.5.cloned.1.call-start
  167.9 108.5 %all-reduce.3.cloned.1.call-done = bf16[1024,2048]{1,0:T(8,128)(2,1)} async-done(((bf16[1024,2048]{1,0:T(8,128)(2,1)}), bf16[1024,2048]{1,0:T(8,128)(2,1)}) %all-reduce.3.cloned.1.call-update) | async-done | bytes 4194320 | tf_op jit(solution)/shard_map/psum | solution.py:99
  276.4 4.8 convert_reduce_fusion.1
  281.1 1.9 copy-done.1
  283.1 1.2 multiply_reduce_fusion
  284.3 44.9 %all-gather.12.cloned.1.call-done = bf16[2,2048,1024]{2,1,0:T(8,128)(2,1)} async-done(((bf16[2,128,1024]{2,1,0:T(8,128)(2,1)}), bf16[2,2048,1024]{2,1,0:T(8,128)(2,1)}) %all-gather.12.cloned.1.call-update) | async-done | bytes 8388624 | tf_op jit(solution)/shard_map/all_gather | solution.py:102
  329.2 14.6 %fusion.23 = f32[2,1024,1024]{2,1,0:T(8,128)} fusion(bf16[2,2048,1024]{2,1,0:T(8,128)(2,1)} %all-gather.12.cloned.1.call-done, bf16[1024,2048]{1,0:T(8,128)(2,1)} %copy-done.1, f32[1024]{0:T(1024)S(1)} %add_rsqrt_fusion, f32[1024]{0:T(1024)S(1)} %broadcast_multiply_fusion), kind=kOutput, calls=%fused_computation.34 | convolution fusion | flops 8598323200 | bytes 20979712 | tf_op jit(solution)/shard_map/td,cdf->ctf/dot_general | solution.py:31
  343.8 32.8 %all-gather.14.cloned.1.call-done = bf16[1024,2048]{1,0:T(8,128)(2,1)} async-done(((bf16[1024,128]{1,0:T(8,128)(2,1)}), bf16[1024,2048]{1,0:T(8,128)(2,1)}) %all-gather.14.cloned.1.call-update) | async-done | bytes 4194320 | tf_op jit(solution)/shard_map/all_gather | solution.py:105
  376.5 11.2 %convolution_convert_fusion.1 = bf16[1024,2048]{1,0:T(8,128)(2,1)} fusion(bf16[1024,2048]{1,0:T(8,128)(2,1)} %all-gather.14.cloned.1.call-done, f32[2,1024,1024]{2,1,0:T(8,128)} %fusion.23), kind=kOutput, calls=%fused_computation.32 | convolution fusion | flops 4303355904 | bytes 16777216 | tf_op jit(solution)/shard_map/dot_general | solution.py:104
  387.7 0.6 copy-done
  388.4 2.0 sort.17
  390.4 0.8 gather_fusion
  391.2 0.7 all_to_all.9
  391.9 4.3 all-to-all-start
  396.2 0.5 copy.34
  396.7 0.2 copy.35
  396.9 0.3 convert_element_type.92
  397.3 0.1 maximum_bitcast_fusion
  397.4 1.6 gather_fusion.1
  398.9 2.7 all-to-all-done
  401.7 4.1 all-to-all-start.1
  405.8 0.1 sub.74
  405.9 45.7 %all-to-all-done.1 = bf16[16,4,2,16,256]{4,3,2,1,0:T(8,128)(2,1)S(1)} async-done(((bf16[16,4,2,16,256]{4,3,2,1,0:T(8,128)(2,1)}), bf16[16,4,2,16,256]{4,3,2,1,0:T(8,128)(2,1)S(1)}, u32[]{:S(2)}, u32[]{:S(2)}) %all-to-all-start.1) | async-done | bytes 1048608 | tf_op jit(solution)/shard_map/all_to_all | solution.py:77
  451.6 0.1 broadcast_in_dim.40
  451.7 2.5 scatter_fusion
  454.2 6.8 %convert_element_type.86 = f32[1024,2048]{1,0:T(8,128)} convert(bf16[1024,2048]{1,0:T(8,128)(2,1)} %copy-done.1) | non-fusion elementwise | flops 2097152 | bytes 12582912 | tf_op jit(solution)/shard_map/convert_element_type | solution.py:108
  461.1 45.0 %all-reduce.5.cloned.1.call-done = bf16[1024,2048]{1,0:T(8,128)(2,1)} async-done(((bf16[1024,2048]{1,0:T(8,128)(2,1)}), bf16[1024,2048]{1,0:T(8,128)(2,1)}) %all-reduce.5.cloned.1.call-update) | async-done | bytes 4194320 | tf_op jit(solution)/shard_map/psum | solution.py:107
  506.1 2.3 fusion.52
  (42 shorter events, 0.5 us)
Async XLA Ops:
  7.2 77.3 %all-gather.6.cloned.1.call-start = ((), (), s32[]{:S(2)}) async-start(), calls=%async_computation.2 | async-start | bytes 4718592 | tf_op jit(solution)/shard_map/all_gather | solution.py:88
  7.9 118.4 %all-gather.8.cloned.1.call-start = ((), (), s32[]{:S(2)}) async-start(), calls=%async_computation.3 | async-start | bytes 3342336 | tf_op jit(solution)/shard_map/all_gather | solution.py:91
  9.7 152.2 %all-gather.10.cloned.1.call-start = ((), (), s32[]{:S(2)}) async-start(), calls=%async_computation.4 | async-start | bytes 1114112 | tf_op jit(solution)/shard_map/all_gather | solution.py:97
  10.4 265.9 %all-reduce.3.cloned.1.call-start = ((), (), s32[]{:S(2)}) async-start(), calls=%async_computation.5 | async-start | bytes 8388608 | tf_op jit(solution)/shard_map/psum | solution.py:99
  84.4 3.4 copy-start.2
  144.4 1.9 copy-start.4
  146.5 0.8 copy-start.7
  147.3 2.9 slice-start
  147.9 1.3 copy-start.6
  149.2 4.5 copy-start.8
  149.2 4.5 copy-start.9
  153.7 3.9 copy-start.5
  166.4 162.8 %all-gather.12.cloned.1.call-start = ((), (), s32[]{:S(2)}) async-start(), calls=%async_computation.6 | async-start | bytes 8912896 | tf_op jit(solution)/shard_map/all_gather | solution.py:102
  167.0 209.5 %all-gather.14.cloned.1.call-start = ((), (), s32[]{:S(2)}) async-start(), calls=%async_computation.7 | async-start | bytes 4456448 | tf_op jit(solution)/shard_map/all_gather | solution.py:105
  167.6 338.5 %all-reduce.5.cloned.1.call-start = ((), (), s32[]{:S(2)}) async-start(), calls=%async_computation.8 | async-start | bytes 8388608 | tf_op jit(solution)/shard_map/psum | solution.py:107
  281.1 1.9 copy-start.1
  387.7 0.7 copy-start
  391.9 9.8 %all-to-all-start = ((s32[16,1,4]{2,1,0:T(1,128)}), s32[16,1,4]{2,1,0:T(1,128)S(1)}, u32[]{:S(2)}, u32[]{:S(2)}) async-start(s32[16,1,4]{2,1,0:T(1,128)} %bitcast.15), calls=%async_computation | async-start | bytes 16384 | tf_op jit(solution)/shard_map/all_to_all | solution.py:78
  401.7 49.9 %all-to-all-start.1 = ((bf16[16,4,2,16,256]{4,3,2,1,0:T(8,128)(2,1)}), bf16[16,4,2,16,256]{4,3,2,1,0:T(8,128)(2,1)S(1)}, u32[]{:S(2)}, u32[]{:S(2)}) async-start(bf16[16,4,2,16,256]{4,3,2,1,0:T(8,128)(2,1)} %bitcast.21), calls=%async_computation.1 | async-start | bytes 2097152 | tf_op jit(solution)/shard_map/all_to_all | solution.py:77
  454.2 6.9 %copy-start.3 = (bf16[64,2,16,256]{3,2,1,0:T(8,128)(2,1)}, bf16[64,2,16,256]{3,2,1,0:T(8,128)(2,1)S(1)}, u32[]{:S(2)}) copy-start(bf16[64,2,16,256]{3,2,1,0:T(8,128)(2,1)S(1)} %scatter_fusion) | copy-start | bytes 3145732
Sparse Core Ops, SparseCore 0:
  10.3 74.0 all-gather.5
  86.6 39.6 all-gather.7
  127.9 33.9 all-gather.9
  166.6 109.7 all-reduce.2
  277.9 51.2 all-gather.11
  330.7 45.8 all-gather.13
  387.9 118.1 all-reduce.4
where the time goes:
time: 516 us; the launch traced here: 515 us
  waiting for transfers between devices  389 us (75%)
  matrix products  47.9 us (9%)
  other arithmetic  29.7 us (6%)
  local copies, waits for them, and re-layouts  25.2 us (5%)
  between operations  14.4 us (3%)
  starting transfers between devices  8.88 us (2%)
    psum x1, waiting for transfers between devices, body(): lax.psum(attn_part.astype(jnp.bfloat16), 'tensor').astype(jnp.float32)  108 us
    all_gather x1, waiting for transfers between devices, body(): full_stream = lax.all_gather(stream, 'tensor', axis=0, tiled=True)  68.2 us
    all_to_all x1, waiting for transfers between devices, write_cache(): lax.all_to_all(outgoing, 'dp', split_axis=0, concat_axis=0, tiled=True)  45.7 us
    psum x1, waiting for transfers between devices, body(): lax.psum(mlp_part.astype(jnp.bfloat16), 'tensor').astype(jnp.float32)  45 us
    all_gather x1, waiting for transfers between devices, body(): lax.all_gather(w_gate_up, 'dp', axis=1, tiled=True)  44.9 us
    all_gather x1, waiting for transfers between devices, body(): lax.all_gather(w_qkv, 'dp', axis=1, tiled=True)  37.2 us
    all_gather x1, waiting for transfers between devices, body(): lax.all_gather(w_down, 'dp', axis=1, tiled=True)  32.8 us
    dot_general x2, matrix products, row_folder(): jnp.einsum('td,cdf->ctf', source, piece, preferred_element_type=jnp.float32)  21.9 us
  transfers between devices with their start and end apart: 9, of which 9 were waited for; matrix products, arithmetic and copies ran while one was open for 15% of the time, Pallas kernels for 0%

commit v1 on v0

--- a/solution.py
+++ b/solution.py
@@ -3,6 +3,7 @@
 import jax.numpy as jnp
 from jax import lax
 from jax.sharding import PartitionSpec as P
+from jax.lax import all_gather
 
 HD = 128
 
@@ -104,7 +105,7 @@
     mlp_part = jnp.dot(
         hidden, lax.all_gather(w_down, "dp", axis=1, tiled=True), preferred_element_type=jnp.float32
     )
-    mlp_whole = lax.psum(mlp_part.astype(jnp.bfloat16), "tensor").astype(jnp.float32)
+    mlp_whole = jnp.sum(all_gather(mlp_part.astype(jnp.bfloat16), "tensor"), 0).astype(jnp.float32)
     result = (mid.astype(jnp.float32) + mlp_whole).astype(jnp.bfloat16)
     layer_out = lax.dynamic_slice_in_dim(
         result, lax.axis_index("tensor") * share_rows, share_rows, 0

time: 516 us -> 762 us (1.48)
  waiting for transfers between devices: 389 us -> 621 us
  other arithmetic: 29.7 us -> 43.8 us
    all_gather x0 -> x1, waiting for transfers between devices: none -> 305 us  [body(): all_gather(mlp_part.astype(jnp.bfloat16), 'tensor')]
    psum x1 -> x0, waiting for transfers between devices: 45 us -> none  [body(): lax.psum(mlp_part.astype(jnp.bfloat16), 'tensor').astype(jnp.float32)]
    all_to_all x1, waiting for transfers between devices: 45.7 us -> 17.3 us  [write_cache(): lax.all_to_all(outgoing, 'dp', split_axis=0, concat_axis=0, tiled=True)]
    reduce_sum x0 -> x1, other arithmetic: none -> 14.1 us  [body(): jnp.sum(all_gather(mlp_part.astype(jnp.bfloat16), 'tensor'), 0)]
  transfers between devices with their start and end apart: 9 -> 9, of which waited for: 9 -> 9; matrix products, arithmetic and copies ran while one was open for 15% -> 10% of each run, Pallas kernels for 0% -> 0%
where the time goes in v1:
time: 762 us; the launch traced here: 761 us
  waiting for transfers between devices  621 us (81%)
  matrix products  47.8 us (6%)
  other arithmetic  43.8 us (6%)
  local copies, waits for them, and re-layouts  25.2 us (3%)
  between operations  14.4 us (2%)
  starting transfers between devices  8.89 us (1%)
    all_gather x1, waiting for transfers between devices, body(): all_gather(mlp_part.astype(jnp.bfloat16), 'tensor')  305 us
    psum x1, waiting for transfers between devices, body(): lax.psum(attn_part.astype(jnp.bfloat16), 'tensor').astype(jnp.float32)  108 us
    all_gather x1, waiting for transfers between devices, body(): full_stream = lax.all_gather(stream, 'tensor', axis=0, tiled=True)  68.2 us
    all_gather x1, waiting for transfers between devices, body(): lax.all_gather(w_gate_up, 'dp', axis=1, tiled=True)  44.9 us
    all_gather x1, waiting for transfers between devices, body(): lax.all_gather(w_qkv, 'dp', axis=1, tiled=True)  37.2 us
    all_gather x1, waiting for transfers between devices, body(): lax.all_gather(w_down, 'dp', axis=1, tiled=True)  32.8 us
    dot_general x2, matrix products, row_folder(): jnp.einsum('td,cdf->ctf', source, piece, preferred_element_type=jnp.float32)  21.9 us
    all_to_all x1, waiting for transfers between devices, write_cache(): lax.all_to_all(outgoing, 'dp', split_axis=0, concat_axis=0, tiled=True)  17.3 us
  transfers between devices with their start and end apart: 9, of which 9 were waited for; matrix products, arithmetic and copies ran while one was open for 10% of the time, Pallas kernels for 0%

profile of v1, /device:TPU:1, one launch (start us, length us, event | category | flops | bytes accessed | tf_op | source)
XLA Modules:
  0.0 761.0 jit_solution(14106033702721702912)
XLA Ops:
  7.2 0.7 all-gather.8.cloned.1.call-update
  7.9 1.7 copy.27
  9.8 0.7 all-gather.12.cloned.1.call-update
  10.5 0.7 convert_element_type.78
  11.2 0.8 fusion.83
  12.0 1.9 multiply_cosine_fusion
  13.9 0.3 compare_and_fusion
  14.2 2.1 fusion.35
  16.2 68.2 %all-gather.8.cloned.1.call-done = bf16[1024,2048]{1,0:T(8,128)(2,1)} async-done(((bf16[128,2048]{1,0:T(8,128)(2,1)}), bf16[1024,2048]{1,0:T(8,128)(2,1)}) %all-gather.8.cloned.1.call-update) | async-done | bytes 4194320 | tf_op jit(solution)/shard_map/all_gather | solution.py:89
  84.4 3.0 convert_reduce_fusion
  87.4 0.5 copy-done.2
  87.9 1.2 fusion.4
  89.1 37.2 %all-gather.10.cloned.1.call-done = bf16[3,2048,256]{1,2,0:T(8,128)(2,1)} async-done(((bf16[3,128,256]{1,2,0:T(8,128)(2,1)}), bf16[3,2048,256]{1,2,0:T(8,128)(2,1)}) %all-gather.10.cloned.1.call-update) | async-done | bytes 3145744 | tf_op jit(solution)/shard_map/all_gather | solution.py:92
  126.3 7.3 fusion.38
  133.6 0.2 fusion.80
  133.9 0.9 slice.112
  134.8 1.0 fusion.81
  135.8 1.4 copy.41
  137.2 2.4 copy.42
  139.5 1.0 fusion.82
  140.6 1.4 copy.39
  141.9 2.4 copy.40
  144.3 1.6 multiply_subtract_fusion
  145.9 0.3 maximum_convert_fusion
  146.2 0.3 subtract_convert_fusion
  146.5 0.8 copy-done.7
  147.3 0.5 fusion.60
  147.8 1.3 copy-done.6
  149.2 1.1 fusion.85
  150.2 3.4 fusion.48
  153.7 3.9 fusion.84
  157.6 2.5 fusion.49
  160.1 1.8 all-gather.12.cloned.1.call-done
  161.9 4.5 convolution_convert_fusion
  166.5 0.5 all-gather.14.cloned.1.call-update
  167.0 0.5 all-gather.16.cloned.1.call-update
  167.6 0.3 all-gather.18.cloned.1.call-start
  167.8 108.4 %all-reduce.2.cloned.1.call-done = bf16[1024,2048]{1,0:T(8,128)(2,1)} async-done(((bf16[1024,2048]{1,0:T(8,128)(2,1)}), bf16[1024,2048]{1,0:T(8,128)(2,1)}) %all-reduce.2.cloned.1.call-update) | async-done | bytes 4194320 | tf_op jit(solution)/shard_map/psum | solution.py:100
  276.2 4.8 convert_reduce_fusion.1
  281.0 1.9 copy-done.1
  282.9 1.2 multiply_reduce_fusion
  284.2 44.9 %all-gather.14.cloned.1.call-done = bf16[2,2048,1024]{2,1,0:T(8,128)(2,1)} async-done(((bf16[2,128,1024]{2,1,0:T(8,128)(2,1)}), bf16[2,2048,1024]{2,1,0:T(8,128)(2,1)}) %all-gather.14.cloned.1.call-update) | async-done | bytes 8388624 | tf_op jit(solution)/shard_map/all_gather | solution.py:103
  329.1 14.6 %fusion.23 = f32[2,1024,1024]{2,1,0:T(8,128)} fusion(bf16[2,2048,1024]{2,1,0:T(8,128)(2,1)} %all-gather.14.cloned.1.call-done, bf16[1024,2048]{1,0:T(8,128)(2,1)} %copy-done.1, f32[1024]{0:T(1024)S(1)} %add_rsqrt_fusion, f32[1024]{0:T(1024)S(1)} %broadcast_multiply_fusion), kind=kOutput, calls=%fused_computation.34 | convolution fusion | flops 8598323200 | bytes 20979712 | tf_op jit(solution)/shard_map/td,cdf->ctf/dot_general | solution.py:32
  343.6 32.8 %all-gather.16.cloned.1.call-done = bf16[1024,2048]{1,0:T(8,128)(2,1)} async-done(((bf16[1024,128]{1,0:T(8,128)(2,1)}), bf16[1024,2048]{1,0:T(8,128)(2,1)}) %all-gather.16.cloned.1.call-update) | async-done | bytes 4194320 | tf_op jit(solution)/shard_map/all_gather | solution.py:106
  376.4 11.2 %convolution_convert_fusion.1 = bf16[1024,2048]{1,0:T(8,128)(2,1)} fusion(bf16[1024,2048]{1,0:T(8,128)(2,1)} %all-gather.16.cloned.1.call-done, f32[2,1024,1024]{2,1,0:T(8,128)} %fusion.23), kind=kOutput, calls=%fused_computation.32 | convolution fusion | flops 4303355904 | bytes 16777216 | tf_op jit(solution)/shard_map/dot_general | solution.py:105
  387.6 0.6 copy-done
  388.2 2.0 sort.17
  390.3 0.8 gather_fusion
  391.0 0.7 all_to_all.9
  391.7 4.3 all-to-all-start
  396.0 0.5 copy.34
  396.6 0.2 copy.35
  396.8 0.3 convert_element_type.94
  397.1 0.1 maximum_bitcast_fusion
  397.2 1.6 gather_fusion.1
  398.8 2.7 all-to-all-done
  401.5 4.1 all-to-all-start.1
  405.7 17.3 %all-to-all-done.1 = bf16[16,4,2,16,256]{4,3,2,1,0:T(8,128)(2,1)S(1)} async-done(((bf16[16,4,2,16,256]{4,3,2,1,0:T(8,128)(2,1)}), bf16[16,4,2,16,256]{4,3,2,1,0:T(8,128)(2,1)S(1)}, u32[]{:S(2)}, u32[]{:S(2)}) %all-to-all-start.1) | async-done | bytes 1048608 | tf_op jit(solution)/shard_map/all_to_all | solution.py:78
  423.0 0.1 broadcast_in_dim.40
  423.1 2.5 scatter_fusion
  425.6 6.8 convert_element_type.88
  432.5 305.4 %all-gather.18.cloned.1.call-done = bf16[8192,2048]{1,0:T(8,128)(2,1)} async-done(((bf16[1024,2048]{1,0:T(8,128)(2,1)}), bf16[8192,2048]{1,0:T(8,128)(2,1)}) %all-gather.18.cloned.1.call-update) | async-done | bytes 33554448 | tf_op jit(solution)/shard_map/all_gather | solution.py:108
  737.8 14.1 %reduce_sum.72 = bf16[1024,2048]{1,0:T(8,128)(2,1)} reduce(bf16[8,1024,2048]{2,1,0:T(8,128)(2,1)} %bitcast.67, bf16[]{:T(256)} %constant.51.clone.1), dimensions={0}, to_apply=%region_9.10 | reduce | flops 14680064 | bytes 37748736 | tf_op jit(solution)/shard_map/reduce_sum | solution.py:108
  751.9 2.3 fusion.52
  (43 shorter events, 0.6 us)
Async XLA Ops:
  7.2 77.3 %all-gather.8.cloned.1.call-start = ((), (), s32[]{:S(2)}) async-start(), calls=%async_computation.2 | async-start | bytes 4718592 | tf_op jit(solution)/shard_map/all_gather | solution.py:89
  7.9 118.4 %all-gather.10.cloned.1.call-start = ((), (), s32[]{:S(2)}) async-start(), calls=%async_computation.3 | async-start | bytes 3342336 | tf_op jit(solution)/shard_map/all_gather | solution.py:92
  9.7 152.2 %all-gather.12.cloned.1.call-start = ((), (), s32[]{:S(2)}) async-start(), calls=%async_computation.4 | async-start | bytes 1114112 | tf_op jit(solution)/shard_map/all_gather | solution.py:98
  10.4 265.8 %all-reduce.2.cloned.1.call-start = ((), (), s32[]{:S(2)}) async-start(), calls=%async_computation.5 | async-start | bytes 8388608 | tf_op jit(solution)/shard_map/psum | solution.py:100
  84.4 3.4 copy-start.2
  144.3 1.9 copy-start.4
  146.5 0.8 copy-start.7
  147.3 3.0 slice-start
  147.8 1.3 copy-start.6
  149.2 4.5 copy-start.8
  149.2 4.5 copy-start.9
  153.6 3.9 copy-start.5
  166.4 162.6 %all-gather.14.cloned.1.call-start = ((), (), s32[]{:S(2)}) async-start(), calls=%async_computation.6 | async-start | bytes 8912896 | tf_op jit(solution)/shard_map/all_gather | solution.py:103
  167.0 209.4 %all-gather.16.cloned.1.call-start = ((), (), s32[]{:S(2)}) async-start(), calls=%async_computation.7 | async-start | bytes 4456448 | tf_op jit(solution)/shard_map/all_gather | solution.py:106
  167.6 570.3 %all-gather.18.cloned.1.call-start = ((), (), s32[]{:S(2)}) async-start(), calls=%async_computation.8 | async-start | bytes 37748736 | tf_op jit(solution)/shard_map/all_gather | solution.py:108
  281.0 1.9 copy-start.1
  387.6 0.7 copy-start
  391.7 9.7 %all-to-all-start = ((s32[16,1,4]{2,1,0:T(1,128)}), s32[16,1,4]{2,1,0:T(1,128)S(1)}, u32[]{:S(2)}, u32[]{:S(2)}) async-start(s32[16,1,4]{2,1,0:T(1,128)} %bitcast.16), calls=%async_computation | async-start | bytes 16384 | tf_op jit(solution)/shard_map/all_to_all | solution.py:79
  401.5 21.5 %all-to-all-start.1 = ((bf16[16,4,2,16,256]{4,3,2,1,0:T(8,128)(2,1)}), bf16[16,4,2,16,256]{4,3,2,1,0:T(8,128)(2,1)S(1)}, u32[]{:S(2)}, u32[]{:S(2)}) async-start(bf16[16,4,2,16,256]{4,3,2,1,0:T(8,128)(2,1)} %bitcast.22), calls=%async_computation.1 | async-start | bytes 2097152 | tf_op jit(solution)/shard_map/all_to_all | solution.py:78
  425.6 6.9 copy-start.3
Sparse Core Ops, SparseCore 0:
  10.3 74.0 all-gather.7
  86.6 39.6 all-gather.9
  127.9 33.9 all-gather.11
  166.5 109.6 all-reduce.1
  277.8 51.2 all-gather.13
  330.5 45.8 all-gather.15
  387.7 350.0 all-gather.17
